TPU v7x, 32 devices: a whole 2x2x4 slice. The times are simulated.
32 devices in a mesh: grp: 2 (over x), date: 16 (over z, y, core).
Axes of the slice: x: 2, y: 2, z: 4, core: 2. Of those that a mesh axis runs over, the one named last changes fastest.
Arguments:
- slc: bfloat16 [16, 2, 128, 2048], P('date', None, 'grp'), parts along dimension 2, may hold values from -6 to 6
- pairs: int32 [64, 2], replicated, may hold values from 0 to 15, as said below
- inverse: bfloat16 [15, 64], replicated, may hold values from -6 to 6
Outputs:
- series: float32 [15, 32, 128], P(None, ('grp', 'date')), parts along dimension 1
There are 2 independent parts, one for each index of `grp`. A program takes and returns all parts, laid end to end along the dimension named above; an argument that names none is the same for every part. Nothing has to cross between parts.
Inputs may be any that keep to these rules, and one draw needn't show every extreme that they name: pairs[p,0] < pairs[p,1] for every pair.
All inputs are finite; a program needn't handle non-finite values.
Results may differ from a plain program's by a relative error of at most 0.0003.
Values may be sent and summed in bfloat16 or wider, within the bound.
No kernel may reach another device: no remote copies, remote signals or barrier semaphores. Data moves between devices by JAX's collectives and lax.ppermute only.
A program may use at most 128 MiB of HBM per device.

v0:
```python
import jax
import jax.numpy as jnp
from jax import lax
from jax.sharding import PartitionSpec as P

LOOK_R = 4
LOOK_C = 16


def coherence(first, second):
    first = first.astype(jnp.float32)
    second = second.astype(jnp.float32)
    cross = first[:, 1] * second[:, 0] - first[:, 0] * second[:, 1]
    power_ref = first[:, 0] * first[:, 0] + first[:, 1] * first[:, 1]
    power_sec = second[:, 0] * second[:, 0] + second[:, 1] * second[:, 1]
    stacked = jnp.stack([cross, power_ref, power_sec])
    three, count, rows, cols = stacked.shape
    rowsum = stacked.reshape(three, count, rows // LOOK_R, LOOK_R, cols).sum(axis=3)
    window = (jnp.arange(cols)[:, None] // LOOK_C == jnp.arange(cols // LOOK_C)[None, :]).astype(
        jnp.float32
    )
    looked = jnp.dot(rowsum, window, precision=lax.Precision.HIGHEST)
    return looked[0] / jnp.sqrt(looked[1] * looked[2] + 1e-06)


def invert(inverse, proxy):
    return jnp.einsum(
        "sp,pxy->sxy", inverse.astype(jnp.float32), proxy, precision=lax.Precision.HIGHEST
    )


def per_device(slc, pairs, inverse):
    stripes = lax.all_to_all(slc, "date", split_axis=2, concat_axis=0, tiled=True)
    first = jnp.take(stripes, pairs[:, 0], axis=0)
    second = jnp.take(stripes, pairs[:, 1], axis=0)
    proxy = coherence(first, second)
    return invert(inverse, proxy)


def solution(mesh):
    in_specs = (P("date", None, "grp", None), P(), P())
    out_specs = P(None, ("grp", "date"), None)
    return jax.shard_map(
        per_device, mesh=mesh, in_specs=in_specs, out_specs=out_specs, check_vma=False
    )
```

profile of v0, /device:TPU:0, one launch (start us, length us, event | category | flops | bytes accessed | tf_op | source)
XLA Modules:
  0.0 41.9 jit_solution(5127418015980830979)
XLA Ops:
  0.0 0.0 copy-start
  0.0 0.0 copy-start.1
  0.0 2.4 %copy.26 = bf16[1,2,64,2048]{3,1,0,2:T(2,128)(2,1)} copy(bf16[1,2,64,2048]{3,2,1,0:T(8,128)(2,1)} %param.5) | data formatting | bytes 1048576 | tf_op args[0]
  2.4 7.4 %all-to-all-start = ((bf16[1,2,64,2048]{3,1,0,2:T(2,128)(2,1)}), bf16[1,2,64,2048]{3,1,0,2:T(2,128)(2,1)S(1)}, u32[]{:S(2)}, u32[]{:S(2)}) async-start(bf16[1,2,64,2048]{3,1,0,2:T(2,128)(2,1)} %copy.26), calls=%async_computation | async-start | bytes 1048576 | tf_op jit(solution)/shard_map/all_to_all | solution.py:33
  9.8 0.0 copy-done.1
  9.9 14.2 %all-to-all-done = bf16[1,2,64,2048]{3,1,0,2:T(2,128)(2,1)S(1)} async-done(((bf16[1,2,64,2048]{3,1,0,2:T(2,128)(2,1)}), bf16[1,2,64,2048]{3,1,0,2:T(2,128)(2,1)S(1)}, u32[]{:S(2)}, u32[]{:S(2)}) %all-to-all-start) | async-done | bytes 524320 | tf_op jit(solution)/shard_map/all_to_all | solution.py:33
  24.1 0.3 copy.38
  24.4 2.4 %gather_fusion = bf16[64,2,4,2048]{3,2,1,0:T(4,128)(2,1)S(1)} fusion(bf16[16,2,4,2048]{3,2,1,0:T(4,128)(2,1)S(1)} %bitcast.30, s32[1024]{0:T(1024)S(1)} %pad_clamp_fusion.1), kind=kCustom, calls=%fused_computation.clone | custom fusion | bytes 4194560 | tf_op jit(solution)/shard_map/jit(_take)/gather | solution.py:34
  26.7 3.6 %gather_fusion.1 = bf16[64,2,4,2048]{3,2,1,0:T(4,128)(2,1)} fusion(bf16[16,2,4,2048]{3,2,1,0:T(4,128)(2,1)S(1)} %bitcast.31, s32[1024]{0:T(1024)S(1)} %pad_clamp_fusion), kind=kCustom, calls=%fused_computation.1.clone | custom fusion | bytes 4194560 | tf_op jit(solution)/shard_map/jit(_take)/gather | solution.py:35
  30.3 7.5 %fusion = (f32[64,2,4,2048]{3,0,2,1:T(8,128)S(1)}, f32[64,2,4,2048]{3,0,2,1:T(8,128)S(1)}) fusion(bf16[64,2,4,2048]{3,2,1,0:T(4,128)(2,1)} %gather_fusion.1, pred[64]{0:T(512)(128)(4,1)S(1)} %get-tuple-element.13, bf16[64,2,4,2048]{3,2,1,0:T(4,128)(2,1)S(1)} %gather_fusion, pred[64]{0:T(512)(128)(4,1)S(1)} %get-tuple-element.6), kind=kLoop, calls=%fused_computation.4 | loop fusion | flops 4194304 | bytes 12583040 | tf_op jit(solution)/shard_map/convert_element_type | solution.py:12
  37.8 1.6 %subtract_bitcast_fusion = (f32[1,64,4,2048]{3,1,2,0:T(8,128)S(1)}, f32[1,64,4,2048]{3,1,2,0:T(8,128)S(1)}, f32[1,64,4,2048]{3,1,2,0:T(8,128)S(1)}) fusion(f32[64,2,4,2048]{3,0,2,1:T(8,128)S(1)} %get-tuple-element.15, f32[64,2,4,2048]{3,0,2,1:T(8,128)S(1)} %get-tuple-element.16), kind=kLoop, calls=%fused_computation.9 | loop fusion | flops 4718592 | bytes 14680064 | tf_op jit(solution)/shard_map/sub | solution.py:13
  39.5 0.7 %maximum_reduce_fusion = f32[3,64,2048]{2,1,0:T(8,128)S(1)} fusion(f32[1,64,4,2048]{3,1,2,0:T(8,128)S(1)} %get-tuple-element.12, f32[1,64,4,2048]{3,1,2,0:T(8,128)S(1)} %get-tuple-element.11, f32[1,64,4,2048]{3,1,2,0:T(8,128)S(1)} %get-tuple-element.10), kind=kLoop, calls=%fused_computation.2 | loop fusion | flops 4325376 | bytes 7864320 | tf_op jit(solution)/shard_map/reduce_sum | solution.py:18
  40.1 1.0 %fusion.3 = f32[3,64,128]{2,1,0:T(8,128)S(1)} fusion(f32[3,64,2048]{2,1,0:T(8,128)S(1)} %maximum_reduce_fusion, s32[2048]{0:T(1024)S(1)} %add_select_fusion), kind=kOutput, calls=%fused_computation.13 | convolution fusion | flops 604241920 | bytes 1679360 | tf_op jit(solution)/shard_map/dot_general | solution.py:22
  41.2 0.0 copy-done
  41.2 0.1 convolution_bitcast_fusion
  41.3 0.6 %copy.30 = f32[15,1,128]{2,1,0:T(1,128)} copy(f32[15,1,128]{2,0,1:T(8,128)S(1)} %convolution_bitcast_fusion) | data formatting | bytes 15360 | tf_op jit(solution)/shard_map/sp,pxy->sxy/dot_general | solution.py:27
  (4 shorter events, 0.0 us)
Async XLA Ops:
  0.0 41.2 %copy-start = (bf16[15,64]{1,0:T(8,128)(2,1)S(1)}, bf16[15,64]{1,0:T(8,128)(2,1)}, u32[]{:S(2)}) copy-start(bf16[15,64]{1,0:T(8,128)(2,1)} %param.7) | copy-start | bytes 5764
  0.0 9.8 %copy-start.1 = (s32[64,2]{0,1:T(2,128)S(1)}, s32[64,2]{0,1:T(2,128)}, u32[]{:S(2)}) copy-start(s32[64,2]{0,1:T(2,128)} %param.6) | copy-start | bytes 1540
  2.4 21.7 %all-to-all-start = ((bf16[1,2,64,2048]{3,1,0,2:T(2,128)(2,1)}), bf16[1,2,64,2048]{3,1,0,2:T(2,128)(2,1)S(1)}, u32[]{:S(2)}, u32[]{:S(2)}) async-start(bf16[1,2,64,2048]{3,1,0,2:T(2,128)(2,1)} %copy.26), calls=%async_computation | async-start | bytes 1048576 | tf_op jit(solution)/shard_map/all_to_all | solution.py:33
where the time goes:
time: 42.2 us; the launch traced here: 41.9 us
  waiting for transfers between devices  14.2 us (34%)
  other arithmetic  9.83 us (23%)
  local copies, waits for them, and re-layouts  9.23 us (22%)
  starting transfers between devices  7.41 us (18%)
  matrix products  1.16 us (3%)
    all_to_all x1, waiting for transfers between devices, per_device(): lax.all_to_all(slc, 'date', split_axis=2, concat_axis=0, tiled=True)  14.2 us
    convert_element_type x1, other arithmetic, coherence(): second = second.astype(jnp.float32)  7.53 us
    all_to_all x1, starting transfers between devices, per_device(): lax.all_to_all(slc, 'date', split_axis=2, concat_axis=0, tiled=True)  7.41 us
    gather x1, local copies, waits for them, and re-layouts, per_device(): second = jnp.take(stripes, pairs[:, 1], axis=0)  3.56 us
    unnamed x5, local copies, waits for them, and re-layouts  2.41 us
    gather x1, local copies, waits for them, and re-layouts, per_device(): first = jnp.take(stripes, pairs[:, 0], axis=0)  2.36 us
    sub x1, other arithmetic, coherence(): cross = first[:, 1] * second[:, 0] - first[:, 0] * second[:, 1]  1.62 us
    dot_general x1, matrix products, coherence(): looked = jnp.dot(rowsum, window, precision=lax.Precision.HIGHEST)  1.03 us
  transfers between devices with their start and end apart: 1, of which 1 were waited for; matrix products, arithmetic and copies ran while one was open for 0% of the time, Pallas kernels for 0%

commit v1 on v0

--- a/solution.py
+++ b/solution.py
@@ -30,7 +30,10 @@
 
 
 def per_device(slc, pairs, inverse):
-    stripes = lax.all_to_all(slc, "date", split_axis=2, concat_axis=0, tiled=True)
+    stripes = jnp.concatenate(
+        lax.all_to_all(jnp.stack(jnp.split(slc, lax.axis_size("date"), axis=2)), "date", 0, 0),
+        axis=0,
+    )
     first = jnp.take(stripes, pairs[:, 0], axis=0)
     second = jnp.take(stripes, pairs[:, 1], axis=0)
     proxy = coherence(first, second)

time: 42.2 us -> 63.7 us (1.51); the launches traced: 41.9 us -> 62.7 us
  local copies, waits for them, and re-layouts: 9.23 us -> 30 us
    unnamed x5 -> x19, local copies, waits for them, and re-layouts: 2.41 us -> 22 us
    another operation x0 -> x1, local copies, waits for them, and re-layouts: none -> 1.47 us  [per_device(): jnp.stack(jnp.split(slc, lax.axis_size('date'), axis=2))]
where the time goes in v1:
time: 63.7 us; the launch traced here: 62.7 us
  local copies, waits for them, and re-layouts  30 us (47%)
  waiting for transfers between devices  14.2 us (22%)
  other arithmetic  9.83 us (15%)
  starting transfers between devices  7.41 us (12%)
  matrix products  1.16 us (2%)
    unnamed x19, local copies, waits for them, and re-layouts  22 us
    all_to_all x1, waiting for transfers between devices, per_device(): lax.all_to_all(jnp.stack(jnp.split(slc, lax.axis_size('date'), axis=2)),...  14.2 us
    convert_element_type x1, other arithmetic, coherence(): second = second.astype(jnp.float32)  7.53 us
    all_to_all x1, starting transfers between devices, per_device(): lax.all_to_all(jnp.stack(jnp.split(slc, lax.axis_size('date'), axis=2)),...  7.41 us
    gather x1, local copies, waits for them, and re-layouts, per_device(): second = jnp.take(stripes, pairs[:, 1], axis=0)  3.56 us
    gather x1, local copies, waits for them, and re-layouts, per_device(): first = jnp.take(stripes, pairs[:, 0], axis=0)  2.36 us
    sub x1, other arithmetic, coherence(): cross = first[:, 1] * second[:, 0] - first[:, 0] * second[:, 1]  1.62 us
    another operation x1, local copies, waits for them, and re-layouts, per_device(): jnp.stack(jnp.split(slc, lax.axis_size('date'), axis=2))  1.47 us
  transfers between devices with their start and end apart: 1, of which 1 were waited for; matrix products, arithmetic and copies ran while one was open for 0% of the time, Pallas kernels for 0%

profile of v1, /device:TPU:0, one launch (start us, length us, event | category | flops | bytes accessed | tf_op | source)
XLA Modules:
  0.0 62.7 jit_solution(13579332644770532090)
XLA Ops:
  0.0 0.0 copy-start
  0.0 0.0 copy-start.1
  0.0 1.5 %constant_dynamic-update-slice_fusion.15 = bf16[16,1,2,4,2048]{4,3,2,1,0:T(4,128)(2,1)} fusion(bf16[1,2,64,2048]{3,2,1,0:T(8,128)(2,1)} %param.5), kind=kLoop, calls=%fused_computation.37 | loop fusion | bytes 65536
  1.5 1.5 %constant_dynamic-update-slice_fusion.14 = bf16[16,1,2,4,2048]{4,3,2,1,0:T(4,128)(2,1)} fusion(bf16[16,1,2,4,2048]{4,3,2,1,0:T(4,128)(2,1)} %constant_dynamic-update-slice_fusion.15, bf16[1,2,64,2048]{3,2,1,0:T(8,128)(2,1)} %param.5), kind=kLoop, calls=%fused_computation.36 | loop fusion | bytes 65536
  3.0 1.5 %constant_dynamic-update-slice_fusion.13 = bf16[16,1,2,4,2048]{4,3,2,1,0:T(4,128)(2,1)} fusion(bf16[16,1,2,4,2048]{4,3,2,1,0:T(4,128)(2,1)} %constant_dynamic-update-slice_fusion.14, bf16[1,2,64,2048]{3,2,1,0:T(8,128)(2,1)} %param.5), kind=kLoop, calls=%fused_computation.35 | loop fusion | bytes 65536
  4.4 1.5 %constant_dynamic-update-slice_fusion.12 = bf16[16,1,2,4,2048]{4,3,2,1,0:T(4,128)(2,1)} fusion(bf16[16,1,2,4,2048]{4,3,2,1,0:T(4,128)(2,1)} %constant_dynamic-update-slice_fusion.13, bf16[1,2,64,2048]{3,2,1,0:T(8,128)(2,1)} %param.5), kind=kLoop, calls=%fused_computation.34 | loop fusion | bytes 65536
  5.9 1.5 %constant_dynamic-update-slice_fusion.11 = bf16[16,1,2,4,2048]{4,3,2,1,0:T(4,128)(2,1)} fusion(bf16[16,1,2,4,2048]{4,3,2,1,0:T(4,128)(2,1)} %constant_dynamic-update-slice_fusion.12, bf16[1,2,64,2048]{3,2,1,0:T(8,128)(2,1)} %param.5), kind=kLoop, calls=%fused_computation.33 | loop fusion | bytes 65536
  7.3 1.5 %constant_dynamic-update-slice_fusion.10 = bf16[16,1,2,4,2048]{4,3,2,1,0:T(4,128)(2,1)} fusion(bf16[16,1,2,4,2048]{4,3,2,1,0:T(4,128)(2,1)} %constant_dynamic-update-slice_fusion.11, bf16[1,2,64,2048]{3,2,1,0:T(8,128)(2,1)} %param.5), kind=kLoop, calls=%fused_computation.32 | loop fusion | bytes 65536
  8.8 1.5 %constant_dynamic-update-slice_fusion.9 = bf16[16,1,2,4,2048]{4,3,2,1,0:T(4,128)(2,1)} fusion(bf16[16,1,2,4,2048]{4,3,2,1,0:T(4,128)(2,1)} %constant_dynamic-update-slice_fusion.10, bf16[1,2,64,2048]{3,2,1,0:T(8,128)(2,1)} %param.5), kind=kLoop, calls=%fused_computation.31 | loop fusion | bytes 65536
  10.3 1.5 %constant_dynamic-update-slice_fusion.8 = bf16[16,1,2,4,2048]{4,3,2,1,0:T(4,128)(2,1)} fusion(bf16[16,1,2,4,2048]{4,3,2,1,0:T(4,128)(2,1)} %constant_dynamic-update-slice_fusion.9, bf16[1,2,64,2048]{3,2,1,0:T(8,128)(2,1)} %param.5), kind=kLoop, calls=%fused_computation.30 | loop fusion | bytes 65536
  11.7 1.5 %constant_dynamic-update-slice_fusion.7 = bf16[16,1,2,4,2048]{4,3,2,1,0:T(4,128)(2,1)} fusion(bf16[16,1,2,4,2048]{4,3,2,1,0:T(4,128)(2,1)} %constant_dynamic-update-slice_fusion.8, bf16[1,2,64,2048]{3,2,1,0:T(8,128)(2,1)} %param.5), kind=kLoop, calls=%fused_computation.29 | loop fusion | bytes 65536
  13.2 1.5 %constant_dynamic-update-slice_fusion.6 = bf16[16,1,2,4,2048]{4,3,2,1,0:T(4,128)(2,1)} fusion(bf16[16,1,2,4,2048]{4,3,2,1,0:T(4,128)(2,1)} %constant_dynamic-update-slice_fusion.7, bf16[1,2,64,2048]{3,2,1,0:T(8,128)(2,1)} %param.5), kind=kLoop, calls=%fused_computation.28 | loop fusion | bytes 65536
  14.7 1.5 %constant_dynamic-update-slice_fusion.5 = bf16[16,1,2,4,2048]{4,3,2,1,0:T(4,128)(2,1)} fusion(bf16[16,1,2,4,2048]{4,3,2,1,0:T(4,128)(2,1)} %constant_dynamic-update-slice_fusion.6, bf16[1,2,64,2048]{3,2,1,0:T(8,128)(2,1)} %param.5), kind=kLoop, calls=%fused_computation.27 | loop fusion | bytes 65536
  16.1 1.5 %constant_dynamic-update-slice_fusion.4 = bf16[16,1,2,4,2048]{4,3,2,1,0:T(4,128)(2,1)} fusion(bf16[16,1,2,4,2048]{4,3,2,1,0:T(4,128)(2,1)} %constant_dynamic-update-slice_fusion.5, bf16[1,2,64,2048]{3,2,1,0:T(8,128)(2,1)} %param.5), kind=kLoop, calls=%fused_computation.26 | loop fusion | bytes 65536
  17.6 1.5 %constant_dynamic-update-slice_fusion.3 = bf16[16,1,2,4,2048]{4,3,2,1,0:T(4,128)(2,1)} fusion(bf16[16,1,2,4,2048]{4,3,2,1,0:T(4,128)(2,1)} %constant_dynamic-update-slice_fusion.4, bf16[1,2,64,2048]{3,2,1,0:T(8,128)(2,1)} %param.5), kind=kLoop, calls=%fused_computation.25 | loop fusion | bytes 65536
  19.1 1.5 %constant_dynamic-update-slice_fusion.2 = bf16[16,1,2,4,2048]{4,3,2,1,0:T(4,128)(2,1)} fusion(bf16[16,1,2,4,2048]{4,3,2,1,0:T(4,128)(2,1)} %constant_dynamic-update-slice_fusion.3, bf16[1,2,64,2048]{3,2,1,0:T(8,128)(2,1)} %param.5), kind=kLoop, calls=%fused_computation.24 | loop fusion | bytes 65536
  20.5 1.5 %constant_dynamic-update-slice_fusion.1 = bf16[16,1,2,4,2048]{4,3,2,1,0:T(4,128)(2,1)} fusion(bf16[16,1,2,4,2048]{4,3,2,1,0:T(4,128)(2,1)} %constant_dynamic-update-slice_fusion.2, bf16[1,2,64,2048]{3,2,1,0:T(8,128)(2,1)} %param.5), kind=kLoop, calls=%fused_computation.23 | loop fusion | bytes 65536
  22.0 1.5 %constant_dynamic-update-slice_fusion = bf16[16,1,2,4,2048]{4,3,2,1,0:T(4,128)(2,1)} fusion(bf16[16,1,2,4,2048]{4,3,2,1,0:T(4,128)(2,1)} %constant_dynamic-update-slice_fusion.1, bf16[1,2,64,2048]{3,2,1,0:T(8,128)(2,1)} %param.5), kind=kLoop, calls=%fused_computation.22 | loop fusion | bytes 65536 | tf_op jit(solution)/shard_map/stack | solution.py:34
  23.5 7.4 %all-to-all-start = ((bf16[16,1,2,4,2048]{4,3,2,1,0:T(4,128)(2,1)}), bf16[16,1,2,4,2048]{4,3,2,1,0:T(4,128)(2,1)S(1)}, u32[]{:S(2)}, u32[]{:S(2)}) async-start(bf16[16,1,2,4,2048]{4,3,2,1,0:T(4,128)(2,1)} %constant_dynamic-update-slice_fusion), calls=%async_computation | async-start | bytes 1048576 | tf_op jit(solution)/shard_map/all_to_all | solution.py:34
  30.9 0.0 copy-done.1
  30.9 14.2 %all-to-all-done = bf16[16,1,2,4,2048]{4,3,2,1,0:T(4,128)(2,1)S(1)} async-done(((bf16[16,1,2,4,2048]{4,3,2,1,0:T(4,128)(2,1)}), bf16[16,1,2,4,2048]{4,3,2,1,0:T(4,128)(2,1)S(1)}, u32[]{:S(2)}, u32[]{:S(2)}) %all-to-all-start) | async-done | bytes 524320 | tf_op jit(solution)/shard_map/all_to_all | solution.py:34
  45.2 2.4 %gather_fusion = bf16[64,2,4,2048]{3,2,1,0:T(4,128)(2,1)S(1)} fusion(bf16[16,2,4,2048]{3,2,1,0:T(4,128)(2,1)S(1)} %bitcast.57, s32[1024]{0:T(1024)S(1)} %pad_clamp_fusion.1), kind=kCustom, calls=%fused_computation.clone | custom fusion | bytes 4194560 | tf_op jit(solution)/shard_map/jit(_take)/gather | solution.py:37
  47.5 3.6 %gather_fusion.1 = bf16[64,2,4,2048]{3,2,1,0:T(4,128)(2,1)} fusion(bf16[16,2,4,2048]{3,2,1,0:T(4,128)(2,1)S(1)} %bitcast.58, s32[1024]{0:T(1024)S(1)} %pad_clamp_fusion), kind=kCustom, calls=%fused_computation.1.clone | custom fusion | bytes 4194560 | tf_op jit(solution)/shard_map/jit(_take)/gather | solution.py:38
  51.1 7.5 %fusion = (f32[64,2,4,2048]{3,0,2,1:T(8,128)S(1)}, f32[64,2,4,2048]{3,0,2,1:T(8,128)S(1)}) fusion(bf16[64,2,4,2048]{3,2,1,0:T(4,128)(2,1)} %gather_fusion.1, pred[64]{0:T(512)(128)(4,1)S(1)} %get-tuple-element.13, bf16[64,2,4,2048]{3,2,1,0:T(4,128)(2,1)S(1)} %gather_fusion, pred[64]{0:T(512)(128)(4,1)S(1)} %get-tuple-element.6), kind=kLoop, calls=%fused_computation.4 | loop fusion | flops 4194304 | bytes 12583040 | tf_op jit(solution)/shard_map/convert_element_type | solution.py:12
  58.6 1.6 %subtract_bitcast_fusion = (f32[1,64,4,2048]{3,1,2,0:T(8,128)S(1)}, f32[1,64,4,2048]{3,1,2,0:T(8,128)S(1)}, f32[1,64,4,2048]{3,1,2,0:T(8,128)S(1)}) fusion(f32[64,2,4,2048]{3,0,2,1:T(8,128)S(1)} %get-tuple-element.15, f32[64,2,4,2048]{3,0,2,1:T(8,128)S(1)} %get-tuple-element.16), kind=kLoop, calls=%fused_computation.9 | loop fusion | flops 4718592 | bytes 14680064 | tf_op jit(solution)/shard_map/sub | solution.py:13
  60.2 0.7 %maximum_reduce_fusion = f32[3,64,2048]{2,1,0:T(8,128)S(1)} fusion(f32[1,64,4,2048]{3,1,2,0:T(8,128)S(1)} %get-tuple-element.12, f32[1,64,4,2048]{3,1,2,0:T(8,128)S(1)} %get-tuple-element.11, f32[1,64,4,2048]{3,1,2,0:T(8,128)S(1)} %get-tuple-element.10), kind=kLoop, calls=%fused_computation.2 | loop fusion | flops 4325376 | bytes 7864320 | tf_op jit(solution)/shard_map/reduce_sum | solution.py:18
  60.9 1.0 %fusion.3 = f32[3,64,128]{2,1,0:T(8,128)S(1)} fusion(f32[3,64,2048]{2,1,0:T(8,128)S(1)} %maximum_reduce_fusion, s32[2048]{0:T(1024)S(1)} %add_select_fusion), kind=kOutput, calls=%fused_computation.13 | convolution fusion | flops 604241920 | bytes 1679360 | tf_op jit(solution)/shard_map/dot_general | solution.py:22
  61.9 0.0 copy-done
  61.9 0.1 convolution_bitcast_fusion
  62.1 0.6 copy.24
  (4 shorter events, 0.0 us)
Async XLA Ops:
  0.0 61.9 %copy-start = (bf16[15,64]{1,0:T(8,128)(2,1)S(1)}, bf16[15,64]{1,0:T(8,128)(2,1)}, u32[]{:S(2)}) copy-start(bf16[15,64]{1,0:T(8,128)(2,1)} %param.7) | copy-start | bytes 5764
  0.0 30.9 %copy-start.1 = (s32[64,2]{0,1:T(2,128)S(1)}, s32[64,2]{0,1:T(2,128)}, u32[]{:S(2)}) copy-start(s32[64,2]{0,1:T(2,128)} %param.6) | copy-start | bytes 1540
  23.5 21.7 %all-to-all-start = ((bf16[16,1,2,4,2048]{4,3,2,1,0:T(4,128)(2,1)}), bf16[16,1,2,4,2048]{4,3,2,1,0:T(4,128)(2,1)S(1)}, u32[]{:S(2)}, u32[]{:S(2)}) async-start(bf16[16,1,2,4,2048]{4,3,2,1,0:T(4,128)(2,1)} %constant_dynamic-update-slice_fusion), calls=%async_computation | async-start | bytes 1048576 | tf_op jit(solution)/shard_map/all_to_all | solution.py:34
